TPU v7x, 32 devices: a whole 2x2x4 slice. The times are simulated.
32 devices in a mesh: groups: 2 (over y), seq: 4 (over z), tensor: 2 (over x), dp: 2 (over core).
Axes of the slice: x: 2, y: 2, z: 4, core: 2. Of those that a mesh axis runs over, the one named last changes fastest.
Arguments:
- tokens: bfloat16 [4, 1024, 4096], P(('groups', 'dp'), 'seq', 'tensor'), parts along dimension 0, may hold values from -6 to 6
- doc_lengths: int32 [4, 8], P(('groups', 'dp')), parts along dimension 0, may hold values from 1 to 768, 1024 in all within a row
- low_taps: float32 [2, 4096], P(None, 'tensor'), may hold values from 0.66 to 0.75
- high_taps: float32 [2, 4096], P(None, 'tensor'), may hold values from -2.5 to 2.5
- level_weights: float32 [13, 4096], P(None, 'tensor'), may hold values from -2.5 to 2.5
- mix_weight: bfloat16 [4096, 4096], P(None, 'tensor'), may hold values from -0.09375 to 0.09375
- out_grad: bfloat16 [4, 1024, 4096], P(('groups', 'dp'), 'seq', 'tensor'), parts along dimension 0, may hold values from -6 to 6
Outputs:
- result: bfloat16 [4, 1024, 4096], P(('groups', 'dp'), 'seq', 'tensor'), parts along dimension 0
- token_grad: bfloat16 [4, 1024, 4096], P(('groups', 'dp'), 'seq', 'tensor'), parts along dimension 0
- weight_grad: bfloat16 [8192, 4096], P(('groups', 'seq', 'dp'), 'tensor'), parts along dimension 0
- low_grad: float32 [4, 4096], P('groups', 'tensor'), parts along dimension 0
- high_grad: float32 [4, 4096], P('groups', 'tensor'), parts along dimension 0
- level_grad: float32 [26, 4096], P('groups', 'tensor'), parts along dimension 0
There are 2 independent parts, one for each index of `groups`. A program takes and returns all parts, laid end to end along the dimension named above; an argument that names none is the same for every part. Nothing has to cross between parts.
Inputs may be any that keep to these rules, and one draw needn't show every extreme that they name: `doc_lengths`: each row of 8 lengths sums to 1024, and its longest document has exactly 768 positions.
All inputs are finite; a program needn't handle non-finite values.
Results may differ from a plain program's by a relative error of at most 0.015.
Values may be sent and summed in bfloat16 or wider, within the bound.
No kernel may reach another device: no remote copies, remote signals or barrier semaphores. Data moves between devices by JAX's collectives and lax.ppermute only.
A program may use at most 128 MiB of HBM per device.

v0:
```python
import jax
import jax.numpy as jnp
from jax import lax
from jax.sharding import PartitionSpec as P

GELU_SCALE = 0.7978845608028654
GELU_CUBIC = 0.044715


def shifted_2(block, axis, distance):
    devices = range(lax.axis_size(axis))
    route = [(i - distance, i) for i in devices if i - distance in devices]
    return lax.ppermute(block, axis, route)


def gelu_value(values):
    tangent = jnp.tanh(GELU_SCALE * (values + GELU_CUBIC * values * values * values))
    return 0.5 * values * (1.0 + tangent)


def gelu_slope(values):
    tangent = jnp.tanh(GELU_SCALE * (values + GELU_CUBIC * values * values * values))
    return 0.5 * (1.0 + tangent) + 0.5 * values * (1.0 - tangent * tangent) * GELU_SCALE * (
        1.0 + 3.0 * GELU_CUBIC * values * values
    )


def doc_starts(positions, doc_lengths):
    bounds = jnp.cumsum(doc_lengths, axis=1) - doc_lengths
    before = bounds[:, None, :] <= positions[None, :, None]
    return jnp.max(jnp.where(before, bounds[:, None, :], -1), axis=2)


def tap_mask(positions, starts, spacing):
    return (positions[None, :] - spacing >= starts)[:, :, None]


def shards(tokens, doc_lengths, low_taps, high_taps, level_weights, mix_weight, out_grad):
    batch_size, row_count, channels = tokens.shape
    levels = level_weights.shape[0] - 1
    seq_count = lax.axis_size("seq")
    core_count = lax.axis_size("dp")
    grad_scale = float(batch_size * row_count * seq_count * core_count) ** (-0.5)
    offset = lax.axis_index("seq") * row_count
    positions = offset + jnp.arange(row_count, dtype=jnp.int32)
    starts = doc_starts(positions, doc_lengths)
    shallow = min(levels, row_count.bit_length() - 1)
    summed = jnp.zeros(tokens.shape, jnp.float32)
    states = [tokens]
    previous_list = []
    current = tokens
    for level_index in range(shallow):
        spacing = 2**level_index
        border = shifted_2(current[:, row_count - spacing :, :], "seq", 1)
        shifted = jnp.concatenate([border, current[:, : row_count - spacing, :]], axis=1)
        previous = jnp.where(tap_mask(positions, starts, spacing), shifted, jnp.zeros_like(shifted))
        summed = summed + level_weights[level_index] * (
            high_taps[0] * previous + high_taps[1] * current
        )
        current = (low_taps[0] * previous + low_taps[1] * current).astype(jnp.bfloat16)
        previous_list.append(previous)
        states.append(current)
    for level_index in range(shallow, levels):
        spacing = 2**level_index
        device_hops = spacing // row_count
        if device_hops < seq_count:
            shifted = shifted_2(current, "seq", device_hops)
        else:
            shifted = jnp.zeros_like(current)
        previous = jnp.where(tap_mask(positions, starts, spacing), shifted, jnp.zeros_like(shifted))
        summed = summed + level_weights[level_index] * (
            high_taps[0] * previous + high_taps[1] * current
        )
        current = (low_taps[0] * previous + low_taps[1] * current).astype(jnp.bfloat16)
        previous_list.append(previous)
        states.append(current)
    summed = summed + level_weights[levels] * current
    activated = gelu_value(summed).astype(jnp.bfloat16)
    partial_mix = jnp.einsum(
        "brc,oc->bro", activated, mix_weight, preferred_element_type=jnp.float32
    )
    mixed = lax.psum_scatter(
        partial_mix.astype(jnp.bfloat16), "tensor", scatter_dimension=2, tiled=True
    ).astype(jnp.float32)
    result = (tokens.astype(jnp.float32) + mixed).astype(jnp.bfloat16)
    gathered = lax.all_gather(out_grad, "tensor", axis=2, tiled=True)
    act_grad = jnp.einsum("bro,oc->brc", gathered, mix_weight, preferred_element_type=jnp.float32)
    weight_grad = lax.psum_scatter(
        (
            jnp.einsum("bro,brc->oc", gathered, activated, preferred_element_type=jnp.float32)
            * grad_scale
        ).astype(jnp.bfloat16),
        ("seq", "dp"),
        scatter_dimension=0,
        tiled=True,
    )
    summed_grad = act_grad * gelu_slope(summed)
    carry_grad = (level_weights[levels] * summed_grad).astype(jnp.bfloat16)
    weight_sums = [None] * (levels + 1)
    weight_sums[levels] = jnp.sum(summed_grad * states[levels].astype(jnp.float32), axis=(0, 1))
    low_first = jnp.zeros((channels,), jnp.float32)
    low_second = jnp.zeros((channels,), jnp.float32)
    high_first = jnp.zeros((channels,), jnp.float32)
    high_second = jnp.zeros((channels,), jnp.float32)
    for level_index in range(levels - 1, -1, -1):
        spacing = 2**level_index
        current = states[level_index]
        previous = previous_list[level_index]
        weighted = level_weights[level_index] * summed_grad
        highpass = high_taps[0] * previous + high_taps[1] * current
        weight_sums[level_index] = jnp.sum(summed_grad * highpass, axis=(0, 1))
        grad_wide = carry_grad.astype(jnp.float32)
        low_first = low_first + jnp.sum(grad_wide * previous.astype(jnp.float32), axis=(0, 1))
        low_second = low_second + jnp.sum(grad_wide * current.astype(jnp.float32), axis=(0, 1))
        high_first = high_first + jnp.sum(weighted * previous.astype(jnp.float32), axis=(0, 1))
        high_second = high_second + jnp.sum(weighted * current.astype(jnp.float32), axis=(0, 1))
        carried = low_taps[0] * carry_grad + high_taps[0] * weighted
        stayed = low_taps[1] * carry_grad + high_taps[1] * weighted
        outgoing = jnp.where(
            tap_mask(positions, starts, spacing), carried, jnp.zeros_like(carried)
        ).astype(jnp.bfloat16)
        if level_index < shallow:
            border = shifted_2(outgoing[:, :spacing, :], "seq", -1)
            pulled = jnp.concatenate([outgoing[:, spacing:, :], border], axis=1)
        else:
            device_hops = spacing // row_count
            if device_hops < seq_count:
                pulled = shifted_2(outgoing, "seq", -device_hops)
            else:
                pulled = jnp.zeros_like(outgoing)
        carry_grad = (stayed + pulled).astype(jnp.bfloat16)
    token_grad = (out_grad.astype(jnp.float32) + carry_grad.astype(jnp.float32)).astype(
        jnp.bfloat16
    )
    low_grad = jnp.stack([low_first, low_second]) * grad_scale
    high_grad = jnp.stack([high_first, high_second]) * grad_scale
    level_grad = jnp.stack(weight_sums) * grad_scale
    low_grad, high_grad, level_grad = (
        lax.psum(low_grad.astype(jnp.bfloat16), ("seq", "dp")).astype(jnp.float32),
        lax.psum(high_grad.astype(jnp.bfloat16), ("seq", "dp")).astype(jnp.float32),
        lax.psum(level_grad.astype(jnp.bfloat16), ("seq", "dp")).astype(jnp.float32),
    )
    return (result, token_grad, weight_grad, low_grad, high_grad, level_grad)


def solution(mesh):
    placed = (
        P(("groups", "dp"), "seq", "tensor"),
        P(("groups", "dp"), None),
        P(None, "tensor"),
        P(None, "tensor"),
        P(None, "tensor"),
        P(None, "tensor"),
        P(("groups", "dp"), "seq", "tensor"),
    )
    return jax.shard_map(
        shards,
        mesh=mesh,
        in_specs=placed,
        out_specs=(
            P(("groups", "dp"), "seq", "tensor"),
            P(("groups", "dp"), "seq", "tensor"),
            P(("groups", "seq", "dp"), "tensor"),
            P("groups", "tensor"),
            P("groups", "tensor"),
            P("groups", "tensor"),
        ),
        check_vma=False,
    )
```

profile of v0, /device:TPU:0, one launch (start us, length us, event | category | flops | bytes accessed | tf_op | source)
XLA Modules:
  0.0 565.9 jit_solution(1448448901782919432)
XLA Ops:
  8.0 4.9 collective-permute-start
  23.9 4.2 collective-permute-start.2
  30.2 4.2 collective-permute-start.3
  36.7 4.2 collective-permute-start.4
  43.4 4.3 collective-permute-start.5
  51.8 4.4 collective-permute-start.6
  56.3 6.0 %collective-permute-done.6 = bf16[1,64,2048]{2,1,0:T(8,128)(2,1)S(1)} collective-permute-done((bf16[1,64,2048]{2,1,0:T(8,128)(2,1)S(1)}, bf16[1,64,2048]{2,1,0:T(8,128)(2,1)S(1)}, u32[]{:S(2)}, u32[]{:S(2)}) %collective-permute-start.6) | collective-permute-done | bytes 262176 | tf_op jit(solution)/shard_map/ppermute | solution.py:13
  63.0 4.4 collective-permute-start.7
  67.4 8.8 %collective-permute-done.7 = bf16[1,128,2048]{2,1,0:T(8,128)(2,1)S(1)} collective-permute-done((bf16[1,128,2048]{2,1,0:T(8,128)(2,1)S(1)}, bf16[1,128,2048]{2,1,0:T(8,128)(2,1)S(1)}, u32[]{:S(2)}, u32[]{:S(2)}) %collective-permute-start.7) | collective-permute-done | bytes 524320 | tf_op jit(solution)/shard_map/ppermute | solution.py:13
  77.7 5.5 collective-permute-start.8
  83.5 14.6 %collective-permute-done.8 = bf16[1,256,2048]{2,1,0:T(8,128)(2,1)} collective-permute-done((bf16[1,256,2048]{2,1,0:T(8,128)(2,1)}, bf16[1,256,2048]{2,1,0:T(8,128)(2,1)}, u32[]{:S(2)}, u32[]{:S(2)}) %collective-permute-start.8) | collective-permute-done | bytes 1048608 | tf_op jit(solution)/shard_map/ppermute | solution.py:13
  100.2 17.4 %collective-permute-start.9 = (bf16[1,256,2048]{2,1,0:T(8,128)(2,1)S(1)}, bf16[1,256,2048]{2,1,0:T(8,128)(2,1)S(1)}, u32[]{:S(2)}, u32[]{:S(2)}) collective-permute-start(bf16[1,256,2048]{2,1,0:T(8,128)(2,1)S(1)} %fusion.57), channel_id=1, source_target_pairs={{0,8},{4,12},{1,9},{5,13},{2,10},{6,14},{3,11},{7,15},{16,24},{20,... | collective-permute-start | bytes 3145736 | tf_op jit(solution)/shard_map/ppermute | solution.py:13
  119.4 10.2 %collective-permute-done.9 = bf16[1,256,2048]{2,1,0:T(8,128)(2,1)S(1)} collective-permute-done((bf16[1,256,2048]{2,1,0:T(8,128)(2,1)S(1)}, bf16[1,256,2048]{2,1,0:T(8,128)(2,1)S(1)}, u32[]{:S(2)}, u32[]{:S(2)}) %collective-permute-start.9) | collective-permute-done | bytes 1048608 | tf_op jit(solution)/shard_map/ppermute | solution.py:13
  130.9 13.8 %fusion.3 = (f32[1,256,2048]{2,1,0:T(8,128)}, bf16[1,256,2048]{2,1,0:T(8,128)(2,1)}) fusion(bf16[1,256,2048]{2,1,0:T(8,128)(2,1)S(1)} %fusion.57, bf16[1,256,2048]{2,1,0:T(8,128)(2,1)} %fusion.52, bf16[1,256,2048]{2,1,0:T(8,128)(2,1)} %copy-done.15, bf16[1,256,2048]{2,1,0:T(8,128)(2,1)} %copy-done.13, bf16[1,256,2048]{2,1,0:T(8,128)(2,1)S(1)} %copy-done.11, ...), kind=kLoop, calls=%fused_computation.123 | loop fusion | flops 70254592 | bytes 24275456 | tf_op jit(solution)/shard_map/add | solution.py:77
  144.8 11.1 %fusion.88 = (bf16[1,256,2048]{2,1,0:T(8,128)(2,1)S(1)}, f32[1,256,2048]{2,1,0:T(8,128)S(1)}) fusion(f32[2048]{0:T(1024)} %bitcast.180, f32[2048]{0:T(1024)S(1)} %bitcast.105, f32[2048]{0:T(1024)} %bitcast.133, pred[256]{0:T(512)(128)(4,1)} %get-tuple-element.139, f32[2048]{0:T(1024)} %bitcast.177, f32[2048]{0:T(1024)} %bitcast.186, f32[2048]{0:T(1024)} %bitcast.116, ...), kind=kOutput, calls=%fused_computation.208 | convolution fusion | flops 4315414528 | bytes 24183040 | tf_op jit(solution)/shard_map/bro,oc->brc/dot_general | solution.py:87
  157.2 38.8 %collective-permute-done.10 = bf16[1,256,2048]{2,1,0:T(8,128)(2,1)S(1)} collective-permute-done((bf16[1,256,2048]{2,1,0:T(8,128)(2,1)S(1)}, bf16[1,256,2048]{2,1,0:T(8,128)(2,1)S(1)}, u32[]{:S(2)}, u32[]{:S(2)}) %collective-permute-start.10) | collective-permute-done | bytes 1048608 | tf_op jit(solution)/shard_map/ppermute | solution.py:13
  196.1 8.5 %fusion.4 = (f32[2048]{0:T(1024)}, f32[2048]{0:T(1024)}, f32[2048]{0:T(1024)}, f32[2048]{0:T(1024)}, f32[2048]{0:T(1024)}, /*index=5*/f32[2048]{0:T(1024)}, f32[...) fusion(f32[1,256,2048]{2,1,0:T(8,128)S(1)} %get-tuple-element.1, ...), kind=kLoop, calls=%fused_computation.124 | loop fusion | flops 47667200 | bytes 9691648 | tf_op jit(solution)/shard_map/reduce_sum | solution.py:100
  206.5 21.0 %collective-permute-done.11 = bf16[1,256,2048]{2,1,0:T(8,128)(2,1)S(1)} collective-permute-done((bf16[1,256,2048]{2,1,0:T(8,128)(2,1)S(1)}, bf16[1,256,2048]{2,1,0:T(8,128)(2,1)S(1)}, u32[]{:S(2)}, u32[]{:S(2)}) %collective-permute-start.11) | collective-permute-done | bytes 1048608 | tf_op jit(solution)/shard_map/ppermute | solution.py:13
  231.3 12.4 %collective-permute-done.12 = bf16[1,128,2048]{2,1,0:T(8,128)(2,1)S(1)} collective-permute-done((bf16[1,128,2048]{2,1,0:T(8,128)(2,1)S(1)}, bf16[1,128,2048]{2,1,0:T(8,128)(2,1)S(1)}, u32[]{:S(2)}, u32[]{:S(2)}) %collective-permute-start.12) | collective-permute-done | bytes 524320 | tf_op jit(solution)/shard_map/ppermute | solution.py:13
  245.2 4.6 multiply_reduce_fusion.2
  251.3 6.9 %collective-permute-done.13 = bf16[1,64,2048]{2,1,0:T(8,128)(2,1)S(1)} collective-permute-done((bf16[1,64,2048]{2,1,0:T(8,128)(2,1)S(1)}, bf16[1,64,2048]{2,1,0:T(8,128)(2,1)S(1)}, u32[]{:S(2)}, u32[]{:S(2)}) %collective-permute-start.13) | collective-permute-done | bytes 262176 | tf_op jit(solution)/shard_map/ppermute | solution.py:13
  263.0 12.5 %fusion.1 = bf16[1,256,4096]{2,1,0:T(8,128)(2,1)} fusion(bf16[4096,2048]{1,0:T(8,128)(2,1)} %param.12, f32[1,256,2048]{2,1,0:T(8,128)} %get-tuple-element.111), kind=kOutput, calls=%fused_computation.3 | convolution fusion | flops 4300734464 | bytes 20971520 | tf_op jit(solution)/shard_map/brc,oc->bro/dot_general | solution.py:79
  285.1 5.4 collective-permute-done.15
  293.4 4.4 collective-permute-done.16
  298.8 4.1 multiply_reduce_fusion.6
  304.6 4.1 collective-permute-done.17
  318.4 7.1 %multiply_reduce_fusion.8 = (f32[2048]{0:T(1024)}, f32[2048]{0:T(1024)}, f32[2048]{0:T(1024)}, f32[2048]{0:T(1024)}, f32[2048]{0:T(1024)}, /*index=5*/f32[2048]{...) fusion(f32[1,256,2048]{2,1,0:T(8,128)S(1)} %get-tuple-element.150, ...), kind=kLoop, calls=%fused_computation.295 | loop fusion | flops 25149440 | bytes 11641344 | tf_op jit(solution)/shard_map/reduce_sum | solution.py:111
  331.7 13.1 %fusion = bf16[4096,2048]{0,1:T(8,128)(2,1)} fusion(bf16[1,256,4096]{2,1,0:T(8,128)(2,1)} %all-gather.2.cloned.1.call-done, f32[1,256,2048]{2,1,0:T(8,128)} %get-tuple-element.111), kind=kOutput, calls=%fused_computation.1 | convolution fusion | flops 4316463104 | bytes 20971520 | tf_op jit(solution)/shard_map/bro,brc->oc/dot_general | solution.py:90
  347.5 4.0 collective-permute-done.19
  353.3 28.3 %all-reduce.3.cloned.1.call-done = (bf16[2,2048]{1,0:T(2,128)(2,1)}, bf16[2,2048]{1,0:T(2,128)(2,1)}, bf16[13,2048]{1,0:T(8,128)(2,1)}) async-done(((bf16[2,2048]{1,0:T(2,128)(2,1)}, bf16[2,2048]{1,0:T(2,128)(2,1)}, bf16[13,2048]{1,0:T(8,128)(2,1)}), (bf16[2,2048]{1,0:T(2,128)(2,1)}, bf16[2,2048]{1,0:T(2,128)(2,1)}, bf16[13,2048]{1,0:T(8,128)(2,1)})) %all-reduce.3.cloned.1.call-update) | async-done | bytes 69648 | tf_op jit(solution)/shard_map/psum | solution.py:139
  385.7 169.5 %reduce-scatter.5.cloned.1.call-done = bf16[512,2048]{0,1:T(8,128)(2,1)} async-done(((bf16[4096,2048]{0,1:T(8,128)(2,1)}), bf16[512,2048]{0,1:T(8,128)(2,1)}) %reduce-scatter.5.cloned.1.call-update) | async-done | bytes 2097168 | tf_op jit(solution)/shard_map/reduce_scatter | solution.py:88
  555.2 3.9 copy.14
  (412 shorter events, 83.2 us)
Async XLA Ops:
  7.2 137.5 %all-gather.2.cloned.1.call-start = ((), (), s32[]{:S(2)}) async-start(), calls=%async_computation.3 | async-start | bytes 3145728 | tf_op jit(solution)/shard_map/all_gather | solution.py:86
  8.0 8.0 %collective-permute-start = (bf16[1,1,2048]{2,1,0:T(2,128)(2,1)S(1)}, bf16[1,1,2048]{2,1,0:T(2,128)(2,1)S(1)}, u32[]{:S(2)}, u32[]{:S(2)}) collective-permute-start(bf16[1,1,2048]{2,1,0:T(2,128)(2,1)S(1)} %slice.100), channel_id=1, source_target_pairs={{0,4},{4,8},{8,12},{1,5},{5,9},{9,13},{2,6},{6,10},{10,14},{3,7},{... | collective-permute-start | bytes 12296 | tf_op jit(solution)/shard_map/ppermute | solution.py:13
  16.0 60.2 %copy-start.133 = (pred[256]{0:T(512)(128)(4,1)}, pred[256]{0:T(512)(128)(4,1)S(1)}, u32[]{:S(2)}) copy-start(pred[256]{0:T(512)(128)(4,1)S(1)} %get-tuple-element.141) | copy-start | bytes 772
  18.3 111.4 %copy-start = (bf16[1,256,2048]{2,1,0:T(8,128)(2,1)}, bf16[1,256,2048]{2,1,0:T(8,128)(2,1)S(1)}, u32[]{:S(2)}) copy-start(bf16[1,256,2048]{2,1,0:T(8,128)(2,1)S(1)} %fusion.18) | copy-start | bytes 3145732
  18.3 4.8 collective-permute-start.1
  23.9 5.6 collective-permute-start.2
  30.2 5.8 %collective-permute-start.3 = (bf16[1,8,2048]{2,1,0:T(8,128)(2,1)S(1)}, bf16[1,8,2048]{2,1,0:T(8,128)(2,1)S(1)}, u32[]{:S(2)}, u32[]{:S(2)}) collective-permute-start(bf16[1,8,2048]{2,1,0:T(8,128)(2,1)S(1)} %slice.151), channel_id=1, source_target_pairs={{0,4},{4,8},{8,12},{1,5},{5,9},{9,13},{2,6},{6,10},{10,14},{3,7},{... | collective-permute-start | bytes 98312 | tf_op jit(solution)/shard_map/ppermute | solution.py:13
  36.7 6.1 %collective-permute-start.4 = (bf16[1,16,2048]{2,1,0:T(8,128)(2,1)S(1)}, bf16[1,16,2048]{2,1,0:T(8,128)(2,1)S(1)}, u32[]{:S(2)}, u32[]{:S(2)}) collective-permute-start(bf16[1,16,2048]{2,1,0:T(8,128)(2,1)S(1)} %slice.153), channel_id=1, source_target_pairs={{0,4},{4,8},{8,12},{1,5},{5,9},{9,13},{2,6},{6,10},{10,14},{3,7},{... | collective-permute-start | bytes 196616 | tf_op jit(solution)/shard_map/ppermute | solution.py:13
  43.4 7.8 %collective-permute-start.5 = (bf16[1,32,2048]{2,1,0:T(8,128)(2,1)S(1)}, bf16[1,32,2048]{2,1,0:T(8,128)(2,1)S(1)}, u32[]{:S(2)}, u32[]{:S(2)}) collective-permute-start(bf16[1,32,2048]{2,1,0:T(8,128)(2,1)S(1)} %slice.155), channel_id=1, source_target_pairs={{0,4},{4,8},{8,12},{1,5},{5,9},{9,13},{2,6},{6,10},{10,14},{3,7},{... | collective-permute-start | bytes 393224 | tf_op jit(solution)/shard_map/ppermute | solution.py:13
  51.8 10.5 %collective-permute-start.6 = (bf16[1,64,2048]{2,1,0:T(8,128)(2,1)S(1)}, bf16[1,64,2048]{2,1,0:T(8,128)(2,1)S(1)}, u32[]{:S(2)}, u32[]{:S(2)}) collective-permute-start(bf16[1,64,2048]{2,1,0:T(8,128)(2,1)S(1)} %slice.157), channel_id=1, source_target_pairs={{0,4},{4,8},{8,12},{1,5},{5,9},{9,13},{2,6},{6,10},{10,14},{3,7},{... | collective-permute-start | bytes 786440 | tf_op jit(solution)/shard_map/ppermute | solution.py:13
  63.0 13.2 %collective-permute-start.7 = (bf16[1,128,2048]{2,1,0:T(8,128)(2,1)S(1)}, bf16[1,128,2048]{2,1,0:T(8,128)(2,1)S(1)}, u32[]{:S(2)}, u32[]{:S(2)}) collective-permute-start(bf16[1,128,2048]{2,1,0:T(8,128)(2,1)S(1)} %get-tuple-element.120), channel_id=1, source_target_pairs={{0,4},{4,8},{8,12},{1,5},{5,9},{9,13},{2,6},{6,10},{10,14},{3,7},{... | collective-permute-start | bytes 1572872 | tf_op jit(solution)/shard_map/ppermute | solution.py:13
  77.7 53.0 %copy-start.2 = (bf16[1,256,2048]{2,1,0:T(8,128)(2,1)S(1)}, bf16[1,256,2048]{2,1,0:T(8,128)(2,1)}, u32[]{:S(2)}) copy-start(bf16[1,256,2048]{2,1,0:T(8,128)(2,1)} %param.7) | copy-start | bytes 3145732
  77.7 20.4 %collective-permute-start.8 = (bf16[1,256,2048]{2,1,0:T(8,128)(2,1)}, bf16[1,256,2048]{2,1,0:T(8,128)(2,1)}, u32[]{:S(2)}, u32[]{:S(2)}) collective-permute-start(bf16[1,256,2048]{2,1,0:T(8,128)(2,1)} %fusion.52), channel_id=1, source_target_pairs={{0,4},{4,8},{8,12},{1,5},{5,9},{9,13},{2,6},{6,10},{10,14},{3,7},{... | collective-permute-start | bytes 3145736 | tf_op jit(solution)/shard_map/ppermute | solution.py:13
  83.2 234.9 %reduce-scatter.3.cloned.1.call-start = ((), (), s32[]{:S(2)}) async-start(), calls=%async_computation.2 | async-start | bytes 3145728 | tf_op jit(solution)/shard_map/reduce_scatter | solution.py:82
  100.2 29.5 %collective-permute-start.9 = (bf16[1,256,2048]{2,1,0:T(8,128)(2,1)S(1)}, bf16[1,256,2048]{2,1,0:T(8,128)(2,1)S(1)}, u32[]{:S(2)}, u32[]{:S(2)}) collective-permute-start(bf16[1,256,2048]{2,1,0:T(8,128)(2,1)S(1)} %fusion.57), channel_id=1, source_target_pairs={{0,8},{4,12},{1,9},{5,13},{2,10},{6,14},{3,11},{7,15},{16,24},{20,... | collective-permute-start | bytes 3145736 | tf_op jit(solution)/shard_map/ppermute | solution.py:13
  144.6 51.4 %copy-start.32 = (bf16[1,256,2048]{2,1,0:T(8,128)(2,1)S(1)}, bf16[1,256,2048]{2,1,0:T(8,128)(2,1)}, u32[]{:S(2)}) copy-start(bf16[1,256,2048]{2,1,0:T(8,128)(2,1)} %copy-done.31) | copy-start | bytes 3145732
  144.7 51.4 %copy-start.38 = (bf16[1,256,2048]{2,1,0:T(8,128)(2,1)S(1)}, bf16[1,256,2048]{2,1,0:T(8,128)(2,1)}, u32[]{:S(2)}) copy-start(bf16[1,256,2048]{2,1,0:T(8,128)(2,1)} %copy-done.37) | copy-start | bytes 3145732
  144.7 51.4 %copy-start.39 = (bf16[1,256,2048]{2,1,0:T(8,128)(2,1)S(1)}, bf16[1,256,2048]{2,1,0:T(8,128)(2,1)}, u32[]{:S(2)}) copy-start(bf16[1,256,2048]{2,1,0:T(8,128)(2,1)} %get-tuple-element.112) | copy-start | bytes 3145732
  144.7 51.3 %copy-start.43 = (f32[1,2048]{1,0:T(1,128)S(1)}, f32[1,2048]{1,0:T(1,128)}, u32[]{:S(2)}) copy-start(f32[1,2048]{1,0:T(1,128)} %copy-done.42) | copy-start | bytes 24580
  144.7 51.3 %copy-start.46 = (f32[1,2048]{1,0:T(1,128)S(1)}, f32[1,2048]{1,0:T(1,128)}, u32[]{:S(2)}) copy-start(f32[1,2048]{1,0:T(1,128)} %copy-done.45) | copy-start | bytes 24580
  155.9 40.1 %collective-permute-start.10 = (bf16[1,256,2048]{2,1,0:T(8,128)(2,1)S(1)}, bf16[1,256,2048]{2,1,0:T(8,128)(2,1)S(1)}, u32[]{:S(2)}, u32[]{:S(2)}) collective-permute-start(bf16[1,256,2048]{2,1,0:T(8,128)(2,1)S(1)} %get-tuple-element.149), channel_id=1, source_target_pairs={{8,0},{12,4},{9,1},{13,5},{10,2},{14,6},{11,3},{15,7},{24,16},{28,... | collective-permute-start | bytes 3145736 | tf_op jit(solution)/shard_map/ppermute | solution.py:13
  205.2 22.3 %collective-permute-start.11 = (bf16[1,256,2048]{2,1,0:T(8,128)(2,1)S(1)}, bf16[1,256,2048]{2,1,0:T(8,128)(2,1)S(1)}, u32[]{:S(2)}, u32[]{:S(2)}) collective-permute-start(bf16[1,256,2048]{2,1,0:T(8,128)(2,1)S(1)} %fusion.96), channel_id=1, source_target_pairs={{4,0},{8,4},{12,8},{5,1},{9,5},{13,9},{6,2},{10,6},{14,10},{7,3},{... | collective-permute-start | bytes 3145736 | tf_op jit(solution)/shard_map/ppermute | solution.py:13
  229.6 14.0 %collective-permute-start.12 = (bf16[1,128,2048]{2,1,0:T(8,128)(2,1)S(1)}, bf16[1,128,2048]{2,1,0:T(8,128)(2,1)S(1)}, u32[]{:S(2)}, u32[]{:S(2)}) collective-permute-start(bf16[1,128,2048]{2,1,0:T(8,128)(2,1)S(1)} %get-tuple-element.119), channel_id=1, source_target_pairs={{4,0},{8,4},{12,8},{5,1},{9,5},{13,9},{6,2},{10,6},{14,10},{7,3},{... | collective-permute-start | bytes 1572872 | tf_op jit(solution)/shard_map/ppermute | solution.py:13
  249.8 8.4 %collective-permute-start.13 = (bf16[1,64,2048]{2,1,0:T(8,128)(2,1)S(1)}, bf16[1,64,2048]{2,1,0:T(8,128)(2,1)S(1)}, u32[]{:S(2)}, u32[]{:S(2)}) collective-permute-start(bf16[1,64,2048]{2,1,0:T(8,128)(2,1)S(1)} %slice.164), channel_id=1, source_target_pairs={{4,0},{8,4},{12,8},{5,1},{9,5},{13,9},{6,2},{10,6},{14,10},{7,3},{... | collective-permute-start | bytes 786440 | tf_op jit(solution)/shard_map/ppermute | solution.py:13
  261.7 15.7 %collective-permute-start.14 = (bf16[1,32,2048]{2,1,0:T(8,128)(2,1)}, bf16[1,32,2048]{2,1,0:T(8,128)(2,1)S(1)}, u32[]{:S(2)}, u32[]{:S(2)}) collective-permute-start(bf16[1,32,2048]{2,1,0:T(8,128)(2,1)} %slice.166), channel_id=1, source_target_pairs={{4,0},{8,4},{12,8},{5,1},{9,5},{13,9},{6,2},{10,6},{14,10},{7,3},{... | collective-permute-start | bytes 393224 | tf_op jit(solution)/shard_map/ppermute | solution.py:13
  275.5 106.1 %all-reduce.3.cloned.1.call-start = ((), (), s32[]{:S(2)}) async-start(), calls=%async_computation.5 | async-start | bytes 163840 | tf_op jit(solution)/shard_map/psum | solution.py:139
  283.6 6.9 %collective-permute-start.15 = (bf16[1,16,2048]{2,1,0:T(8,128)(2,1)S(1)}, bf16[1,16,2048]{2,1,0:T(8,128)(2,1)S(1)}, u32[]{:S(2)}, u32[]{:S(2)}) collective-permute-start(bf16[1,16,2048]{2,1,0:T(8,128)(2,1)S(1)} %slice.168), channel_id=1, source_target_pairs={{4,0},{8,4},{12,8},{5,1},{9,5},{13,9},{6,2},{10,6},{14,10},{7,3},{... | collective-permute-start | bytes 196616 | tf_op jit(solution)/shard_map/ppermute | solution.py:13
  292.0 5.8 %collective-permute-start.16 = (bf16[1,8,2048]{2,1,0:T(8,128)(2,1)S(1)}, bf16[1,8,2048]{2,1,0:T(8,128)(2,1)S(1)}, u32[]{:S(2)}, u32[]{:S(2)}) collective-permute-start(bf16[1,8,2048]{2,1,0:T(8,128)(2,1)S(1)} %slice.170), channel_id=1, source_target_pairs={{4,0},{8,4},{12,8},{5,1},{9,5},{13,9},{6,2},{10,6},{14,10},{7,3},{... | collective-permute-start | bytes 98312 | tf_op jit(solution)/shard_map/ppermute | solution.py:13
  302.9 5.8 %collective-permute-start.17 = (bf16[1,4,2048]{2,1,0:T(4,128)(2,1)S(1)}, bf16[1,4,2048]{2,1,0:T(4,128)(2,1)S(1)}, u32[]{:S(2)}, u32[]{:S(2)}) collective-permute-start(bf16[1,4,2048]{2,1,0:T(4,128)(2,1)S(1)} %slice.172), channel_id=1, source_target_pairs={{4,0},{8,4},{12,8},{5,1},{9,5},{13,9},{6,2},{10,6},{14,10},{7,3},{... | collective-permute-start | bytes 49160 | tf_op jit(solution)/shard_map/ppermute | solution.py:13
  310.3 5.7 %collective-permute-start.18 = (bf16[1,2,2048]{2,1,0:T(2,128)(2,1)S(1)}, bf16[1,2,2048]{2,1,0:T(2,128)(2,1)S(1)}, u32[]{:S(2)}, u32[]{:S(2)}) collective-permute-start(bf16[1,2,2048]{2,1,0:T(2,128)(2,1)S(1)} %slice.348), channel_id=1, source_target_pairs={{4,0},{8,4},{12,8},{5,1},{9,5},{13,9},{6,2},{10,6},{14,10},{7,3},{... | collective-permute-start | bytes 24584 | tf_op jit(solution)/shard_map/ppermute | solution.py:13
  331.6 223.6 %reduce-scatter.5.cloned.1.call-start = ((), (), s32[]{:S(2)}) async-start(), calls=%async_computation.4 | async-start | bytes 18874368 | tf_op jit(solution)/shard_map/reduce_scatter | solution.py:88
  346.0 5.6 collective-permute-start.19
  (148 other events, 2426.8 us)
Sparse Core Ops, SparseCore 0:
  83.4 32.4 all-gather.1
  275.6 32.0 reduce-scatter.2
  331.7 49.8 all-reduce.2
  383.8 171.3 reduce-scatter.4
where the time goes:
time: 573 us; the launch traced here: 566 us
  waiting for transfers between devices  348 us (61%)
  other arithmetic  77.7 us (14%)
  starting transfers between devices  71.5 us (12%)
  matrix products  36.7 us (6%)
  between operations  16.3 us (3%)
  local copies, waits for them, and re-layouts  16.1 us (3%)
    reduce_scatter x1, waiting for transfers between devices, shards(): lax.psum_scatter((jnp.einsum('bro,brc->oc', gathered, activated, preferre...  170 us
    ppermute x20, waiting for transfers between devices, shifted_2(): return lax.ppermute(block, axis, route)  150 us
    ppermute x20, starting transfers between devices, shifted_2(): return lax.ppermute(block, axis, route)  70.9 us
    psum x1, waiting for transfers between devices, shards(): lax.psum(low_grad.astype(jnp.bfloat16), ('seq', 'dp')).astype(jnp.float32)  28.3 us
    reduce_sum x4, other arithmetic, shards(): weight_sums[level_index] = jnp.sum(summed_grad * highpass, axis=(0, 1))  19.5 us
    add x1, other arithmetic, shards(): summed = summed + level_weights[levels] * current  13.8 us
    dot_general x1, matrix products, shards(): jnp.einsum('bro,brc->oc', gathered, activated, preferred_element_type=jnp...  13.1 us
    dot_general x1, matrix products, shards(): jnp.einsum('brc,oc->bro', activated, mix_weight, preferred_element_type=j...  12.5 us
  transfers between devices with their start and end apart: 24, of which 20 were waited for; matrix products, arithmetic and copies ran while one was open for 12% of the time, Pallas kernels for 0%

commit v1 on v0

--- a/solution.py
+++ b/solution.py
@@ -5,6 +5,7 @@
 
 GELU_SCALE = 0.7978845608028654
 GELU_CUBIC = 0.044715
+_bind_space = lambda s0: lax.psum(lax.psum(s0, "dp"), "seq")
 
 
 def shifted_2(block, axis, distance):
@@ -136,7 +137,7 @@
     high_grad = jnp.stack([high_first, high_second]) * grad_scale
     level_grad = jnp.stack(weight_sums) * grad_scale
     low_grad, high_grad, level_grad = (
-        lax.psum(low_grad.astype(jnp.bfloat16), ("seq", "dp")).astype(jnp.float32),
+        _bind_space(low_grad.astype(jnp.bfloat16)).astype(jnp.float32),
         lax.psum(high_grad.astype(jnp.bfloat16), ("seq", "dp")).astype(jnp.float32),
         lax.psum(level_grad.astype(jnp.bfloat16), ("seq", "dp")).astype(jnp.float32),
     )

time: 573 us -> 478 us (0.83)
  waiting for transfers between devices: 348 us -> 221 us
  blocking collectives: 0 us -> 40.5 us
  other arithmetic: 77.7 us -> 70.5 us
    reduce_scatter x1, waiting for transfers between devices: 170 us -> 0.01 us  [shards(): lax.psum_scatter((jnp.einsum('bro,brc->oc', gathered, activated, preferre...]
    ppermute x20, waiting for transfers between devices: 150 us -> 221 us  [shifted_2(): return lax.ppermute(block, axis, route)]
    psum x0 -> x3, blocking collectives: none -> 40.5 us  [the longest x1 26.9 us: shards(): lax.psum(high_grad.astype(jnp.bfloat16), ('seq', 'dp')).astype(jnp.float32)]
    psum x1 -> x0, waiting for transfers between devices: 28.3 us -> none  [shards(): lax.psum(low_grad.astype(jnp.bfloat16), ('seq', 'dp')).astype(jnp.float32)]
  transfers between devices with their start and end apart: 24 -> 23, of which waited for: 20 -> 18; matrix products, arithmetic and copies ran while one was open for 12% -> 22% of each run, Pallas kernels for 0% -> 0%
where the time goes in v1:
time: 478 us; the launch traced here: 471 us
  waiting for transfers between devices  221 us (46%)
  starting transfers between devices  71.8 us (15%)
  other arithmetic  70.5 us (15%)
  blocking collectives  40.5 us (8%)
  matrix products  33.6 us (7%)
  local copies, waits for them, and re-layouts  16.8 us (4%)
  between operations  16.5 us (3%)
    ppermute x20, waiting for transfers between devices, shifted_2(): return lax.ppermute(block, axis, route)  221 us
    ppermute x20, starting transfers between devices, shifted_2(): return lax.ppermute(block, axis, route)  71.5 us
    psum x1, blocking collectives, shards(): lax.psum(high_grad.astype(jnp.bfloat16), ('seq', 'dp')).astype(jnp.float32)  26.9 us
    reduce_sum x4, other arithmetic, shards(): weight_sums[level_index] = jnp.sum(summed_grad * highpass, axis=(0, 1))  19.5 us
    add x1, other arithmetic, shards(): summed = summed + level_weights[levels] * current  13.8 us
    psum x2, blocking collectives, _bind_space = lambda s0: lax.psum(lax.psum(s0, 'dp'), 'seq')  13.7 us
    dot_general x1, matrix products, shards(): jnp.einsum('brc,oc->bro', activated, mix_weight, preferred_element_type=j...  12.4 us
    dot_general x1, matrix products, shards(): jnp.einsum('bro,oc->brc', gathered, mix_weight, preferred_element_type=jn...  11.1 us
  transfers between devices with their start and end apart: 23, of which 18 were waited for; matrix products, arithmetic and copies ran while one was open for 22% of the time, Pallas kernels for 0%

profile of v1, /device:TPU:0, one launch (start us, length us, event | category | flops | bytes accessed | tf_op | source)
XLA Modules:
  0.0 470.9 jit_solution(536237196419519168)
XLA Ops:
  8.0 4.9 %collective-permute-start = (bf16[1,1,2048]{2,1,0:T(2,128)(2,1)S(1)}, bf16[1,1,2048]{2,1,0:T(2,128)(2,1)S(1)}, u32[]{:S(2)}, u32[]{:S(2)}) collective-permute-start(bf16[1,1,2048]{2,1,0:T(2,128)(2,1)S(1)} %slice.100), channel_id=1, source_target_pairs={{0,4},{4,8},{8,12},{1,5},{5,9},{9,13},{2,6},{6,10},{10,14},{3,7},{... | collective-permute-start | bytes 12296 | tf_op jit(solution)/shard_map/ppermute | solution.py:14
  23.9 4.2 collective-permute-start.2
  30.3 4.2 collective-permute-start.3
  36.7 4.2 collective-permute-start.4
  43.4 4.3 collective-permute-start.5
  51.8 4.4 collective-permute-start.6
  56.3 6.0 %collective-permute-done.6 = bf16[1,64,2048]{2,1,0:T(8,128)(2,1)S(1)} collective-permute-done((bf16[1,64,2048]{2,1,0:T(8,128)(2,1)S(1)}, bf16[1,64,2048]{2,1,0:T(8,128)(2,1)S(1)}, u32[]{:S(2)}, u32[]{:S(2)}) %collective-permute-start.6) | collective-permute-done | bytes 262176 | tf_op jit(solution)/shard_map/ppermute | solution.py:14
  63.0 4.4 collective-permute-start.7
  67.4 8.8 %collective-permute-done.7 = bf16[1,128,2048]{2,1,0:T(8,128)(2,1)S(1)} collective-permute-done((bf16[1,128,2048]{2,1,0:T(8,128)(2,1)S(1)}, bf16[1,128,2048]{2,1,0:T(8,128)(2,1)S(1)}, u32[]{:S(2)}, u32[]{:S(2)}) %collective-permute-start.7) | collective-permute-done | bytes 524320 | tf_op jit(solution)/shard_map/ppermute | solution.py:14
  77.7 5.6 %collective-permute-start.8 = (bf16[1,256,2048]{2,1,0:T(8,128)(2,1)}, bf16[1,256,2048]{2,1,0:T(8,128)(2,1)}, u32[]{:S(2)}, u32[]{:S(2)}) collective-permute-start(bf16[1,256,2048]{2,1,0:T(8,128)(2,1)} %fusion.52), channel_id=1, source_target_pairs={{0,4},{4,8},{8,12},{1,5},{5,9},{9,13},{2,6},{6,10},{10,14},{3,7},{... | collective-permute-start | bytes 3145736 | tf_op jit(solution)/shard_map/ppermute | solution.py:14
  83.5 14.5 %collective-permute-done.8 = bf16[1,256,2048]{2,1,0:T(8,128)(2,1)} collective-permute-done((bf16[1,256,2048]{2,1,0:T(8,128)(2,1)}, bf16[1,256,2048]{2,1,0:T(8,128)(2,1)}, u32[]{:S(2)}, u32[]{:S(2)}) %collective-permute-start.8) | collective-permute-done | bytes 1048608 | tf_op jit(solution)/shard_map/ppermute | solution.py:14
  100.2 17.7 %collective-permute-start.9 = (bf16[1,256,2048]{2,1,0:T(8,128)(2,1)S(1)}, bf16[1,256,2048]{2,1,0:T(8,128)(2,1)S(1)}, u32[]{:S(2)}, u32[]{:S(2)}) collective-permute-start(bf16[1,256,2048]{2,1,0:T(8,128)(2,1)S(1)} %fusion.57), channel_id=1, source_target_pairs={{0,8},{4,12},{1,9},{5,13},{2,10},{6,14},{3,11},{7,15},{16,24},{20,... | collective-permute-start | bytes 3145736 | tf_op jit(solution)/shard_map/ppermute | solution.py:14
  120.6 9.1 %collective-permute-done.9 = bf16[1,256,2048]{2,1,0:T(8,128)(2,1)S(1)} collective-permute-done((bf16[1,256,2048]{2,1,0:T(8,128)(2,1)S(1)}, bf16[1,256,2048]{2,1,0:T(8,128)(2,1)S(1)}, u32[]{:S(2)}, u32[]{:S(2)}) %collective-permute-start.9) | collective-permute-done | bytes 1048608 | tf_op jit(solution)/shard_map/ppermute | solution.py:14
  129.9 13.8 %fusion.3 = (f32[1,256,2048]{2,1,0:T(8,128)}, bf16[1,256,2048]{2,1,0:T(8,128)(2,1)}) fusion(bf16[1,256,2048]{2,1,0:T(8,128)(2,1)S(1)} %fusion.57, bf16[1,256,2048]{2,1,0:T(8,128)(2,1)} %fusion.52, bf16[1,256,2048]{2,1,0:T(8,128)(2,1)} %copy-done.15, bf16[1,256,2048]{2,1,0:T(8,128)(2,1)} %copy-done.13, bf16[1,256,2048]{2,1,0:T(8,128)(2,1)S(1)} %copy-done.11, ...), kind=kLoop, calls=%fused_computation.123 | loop fusion | flops 70254592 | bytes 24275456 | tf_op jit(solution)/shard_map/add | solution.py:78
  143.8 12.4 %fusion.1 = bf16[1,256,4096]{2,1,0:T(8,128)(2,1)} fusion(bf16[4096,2048]{1,0:T(8,128)(2,1)} %param.12, f32[1,256,2048]{2,1,0:T(8,128)} %get-tuple-element.110), kind=kOutput, calls=%fused_computation.3 | convolution fusion | flops 4300734464 | bytes 20971520 | tf_op jit(solution)/shard_map/brc,oc->bro/dot_general | solution.py:80
  157.9 10.0 %fusion = bf16[4096,2048]{0,1:T(8,128)(2,1)} fusion(bf16[1,256,4096]{2,1,0:T(8,128)(2,1)} %all-gather.2.cloned.1.call-done, f32[1,256,2048]{2,1,0:T(8,128)S(1)} %copy-done.38), kind=kOutput, calls=%fused_computation.1 | convolution fusion | flops 4316463104 | bytes 20971520 | tf_op jit(solution)/shard_map/bro,brc->oc/dot_general | solution.py:91
  168.1 11.1 %fusion.88 = (bf16[1,256,2048]{2,1,0:T(8,128)(2,1)S(1)}, f32[1,256,2048]{2,1,0:T(8,128)S(1)}) fusion(f32[2048]{0:T(1024)} %bitcast.180, f32[2048]{0:T(1024)S(1)} %bitcast.105, f32[2048]{0:T(1024)} %bitcast.133, pred[256]{0:T(512)(128)(4,1)} %get-tuple-element.138, f32[2048]{0:T(1024)} %bitcast.177, f32[2048]{0:T(1024)} %bitcast.186, f32[2048]{0:T(1024)} %bitcast.116, ...), kind=kOutput, calls=%fused_computation.208 | convolution fusion | flops 4315414528 | bytes 24183040 | tf_op jit(solution)/shard_map/bro,oc->brc/dot_general | solution.py:88
  180.5 54.0 %collective-permute-done.10 = bf16[1,256,2048]{2,1,0:T(8,128)(2,1)S(1)} collective-permute-done((bf16[1,256,2048]{2,1,0:T(8,128)(2,1)S(1)}, bf16[1,256,2048]{2,1,0:T(8,128)(2,1)S(1)}, u32[]{:S(2)}, u32[]{:S(2)}) %collective-permute-start.10) | collective-permute-done | bytes 1048608 | tf_op jit(solution)/shard_map/ppermute | solution.py:14
  234.6 8.5 %fusion.4 = (f32[2048]{0:T(1024)}, f32[2048]{0:T(1024)}, f32[2048]{0:T(1024)}, f32[2048]{0:T(1024)}, f32[2048]{0:T(1024)}, /*index=5*/f32[2048]{0:T(1024)}, f32[...) fusion(f32[1,256,2048]{2,1,0:T(8,128)S(1)} %get-tuple-element.1, ...), kind=kLoop, calls=%fused_computation.124 | loop fusion | flops 47667200 | bytes 9691648 | tf_op jit(solution)/shard_map/reduce_sum | solution.py:101
  244.9 49.0 %collective-permute-done.11 = bf16[1,256,2048]{2,1,0:T(8,128)(2,1)S(1)} collective-permute-done((bf16[1,256,2048]{2,1,0:T(8,128)(2,1)S(1)}, bf16[1,256,2048]{2,1,0:T(8,128)(2,1)S(1)}, u32[]{:S(2)}, u32[]{:S(2)}) %collective-permute-start.11) | collective-permute-done | bytes 1048608 | tf_op jit(solution)/shard_map/ppermute | solution.py:14
  297.1 25.1 %collective-permute-done.12 = bf16[1,128,2048]{2,1,0:T(8,128)(2,1)S(1)} collective-permute-done((bf16[1,128,2048]{2,1,0:T(8,128)(2,1)S(1)}, bf16[1,128,2048]{2,1,0:T(8,128)(2,1)S(1)}, u32[]{:S(2)}, u32[]{:S(2)}) %collective-permute-start.12) | collective-permute-done | bytes 524320 | tf_op jit(solution)/shard_map/ppermute | solution.py:14
  323.8 4.5 multiply_reduce_fusion.2
  329.9 14.5 %collective-permute-done.13 = bf16[1,64,2048]{2,1,0:T(8,128)(2,1)S(1)} collective-permute-done((bf16[1,64,2048]{2,1,0:T(8,128)(2,1)S(1)}, bf16[1,64,2048]{2,1,0:T(8,128)(2,1)S(1)}, u32[]{:S(2)}, u32[]{:S(2)}) %collective-permute-start.13) | collective-permute-done | bytes 262176 | tf_op jit(solution)/shard_map/ppermute | solution.py:14
  347.4 9.2 %collective-permute-done.14 = bf16[1,32,2048]{2,1,0:T(8,128)(2,1)S(1)} collective-permute-done((bf16[1,32,2048]{2,1,0:T(8,128)(2,1)S(1)}, bf16[1,32,2048]{2,1,0:T(8,128)(2,1)S(1)}, u32[]{:S(2)}, u32[]{:S(2)}) %collective-permute-start.14) | collective-permute-done | bytes 131104 | tf_op jit(solution)/shard_map/ppermute | solution.py:14
  362.9 6.9 %collective-permute-done.15 = bf16[1,16,2048]{2,1,0:T(8,128)(2,1)S(1)} collective-permute-done((bf16[1,16,2048]{2,1,0:T(8,128)(2,1)S(1)}, bf16[1,16,2048]{2,1,0:T(8,128)(2,1)S(1)}, u32[]{:S(2)}, u32[]{:S(2)}) %collective-permute-start.15) | collective-permute-done | bytes 65568 | tf_op jit(solution)/shard_map/ppermute | solution.py:14
  372.9 5.4 %collective-permute-done.16 = bf16[1,8,2048]{2,1,0:T(8,128)(2,1)S(1)} collective-permute-done((bf16[1,8,2048]{2,1,0:T(8,128)(2,1)S(1)}, bf16[1,8,2048]{2,1,0:T(8,128)(2,1)S(1)}, u32[]{:S(2)}, u32[]{:S(2)}) %collective-permute-start.16) | collective-permute-done | bytes 32800 | tf_op jit(solution)/shard_map/ppermute | solution.py:14
  379.3 4.1 multiply_reduce_fusion.6
  385.1 4.8 %collective-permute-done.17 = bf16[1,4,2048]{2,1,0:T(4,128)(2,1)S(1)} collective-permute-done((bf16[1,4,2048]{2,1,0:T(4,128)(2,1)S(1)}, bf16[1,4,2048]{2,1,0:T(4,128)(2,1)S(1)}, u32[]{:S(2)}, u32[]{:S(2)}) %collective-permute-start.17) | collective-permute-done | bytes 16416 | tf_op jit(solution)/shard_map/ppermute | solution.py:14
  393.2 4.4 collective-permute-done.18
  400.0 7.1 %multiply_reduce_fusion.8 = (f32[2048]{0:T(1024)}, f32[2048]{0:T(1024)}, f32[2048]{0:T(1024)}, f32[2048]{0:T(1024)}, f32[2048]{0:T(1024)}, /*index=5*/f32[2048]{...) fusion(f32[1,256,2048]{2,1,0:T(8,128)S(1)} %get-tuple-element.149, ...), kind=kLoop, calls=%fused_computation.295 | loop fusion | flops 25149440 | bytes 11641344 | tf_op jit(solution)/shard_map/reduce_sum | solution.py:112
  415.1 11.2 %psum.29 = bf16[2,2048]{1,0:T(2,128)(2,1)S(1)} all-reduce(bf16[2,2048]{1,0:T(2,128)(2,1)S(1)} %psum.28), channel_id=1, replica_groups=mesh['groups'=2,'seq'=4,'tensor'=2,'dp'=2] {'seq'}, use_global_device_ids=true, to_apply=%region_29.30 | all-reduce | flops 4096 | bytes 16384 | tf_op jit(solution)/shard_map/psum | solution.py:8
  427.9 26.9 %all-reduce = (bf16[2,2048]{1,0:T(2,128)(2,1)S(1)}, bf16[13,2048]{1,0:T(8,128)(2,1)S(1)}) all-reduce(bf16[2,2048]{1,0:T(2,128)(2,1)S(1)} %fusion.170, bf16[13,2048]{1,0:T(8,128)(2,1)S(1)} %multiply_convert_fusion.3), channel_id=1, replica_groups=mesh['groups'=2,'seq'=4,'tensor'=2,'dp'=2] {'seq','dp'}, use_global_device_ids=true, to_apply=%region_54.55 | all-reduce | flops 30720 | bytes 122880 | tf_op jit(solution)/shard_map/psum | solution.py:141
  (386 shorter events, 79.3 us)
Async XLA Ops:
  7.2 149.4 %all-gather.2.cloned.1.call-start = ((), (), s32[]{:S(2)}) async-start(), calls=%async_computation.3 | async-start | bytes 3145728 | tf_op jit(solution)/shard_map/all_gather | solution.py:87
  8.0 8.0 %collective-permute-start = (bf16[1,1,2048]{2,1,0:T(2,128)(2,1)S(1)}, bf16[1,1,2048]{2,1,0:T(2,128)(2,1)S(1)}, u32[]{:S(2)}, u32[]{:S(2)}) collective-permute-start(bf16[1,1,2048]{2,1,0:T(2,128)(2,1)S(1)} %slice.100), channel_id=1, source_target_pairs={{0,4},{4,8},{8,12},{1,5},{5,9},{9,13},{2,6},{6,10},{10,14},{3,7},{... | collective-permute-start | bytes 12296 | tf_op jit(solution)/shard_map/ppermute | solution.py:14
  18.3 111.4 %copy-start = (bf16[1,256,2048]{2,1,0:T(8,128)(2,1)}, bf16[1,256,2048]{2,1,0:T(8,128)(2,1)S(1)}, u32[]{:S(2)}) copy-start(bf16[1,256,2048]{2,1,0:T(8,128)(2,1)S(1)} %fusion.18) | copy-start | bytes 3145732
  18.3 4.8 %collective-permute-start.1 = (bf16[1,2,2048]{2,1,0:T(2,128)(2,1)S(1)}, bf16[1,2,2048]{2,1,0:T(2,128)(2,1)S(1)}, u32[]{:S(2)}, u32[]{:S(2)}) collective-permute-start(bf16[1,2,2048]{2,1,0:T(2,128)(2,1)S(1)} %slice.147), channel_id=1, source_target_pairs={{0,4},{4,8},{8,12},{1,5},{5,9},{9,13},{2,6},{6,10},{10,14},{3,7},{... | collective-permute-start | bytes 24584 | tf_op jit(solution)/shard_map/ppermute | solution.py:14
  23.9 5.6 %collective-permute-start.2 = (bf16[1,4,2048]{2,1,0:T(4,128)(2,1)S(1)}, bf16[1,4,2048]{2,1,0:T(4,128)(2,1)S(1)}, u32[]{:S(2)}, u32[]{:S(2)}) collective-permute-start(bf16[1,4,2048]{2,1,0:T(4,128)(2,1)S(1)} %slice.149), channel_id=1, source_target_pairs={{0,4},{4,8},{8,12},{1,5},{5,9},{9,13},{2,6},{6,10},{10,14},{3,7},{... | collective-permute-start | bytes 49160 | tf_op jit(solution)/shard_map/ppermute | solution.py:14
  30.3 5.8 %collective-permute-start.3 = (bf16[1,8,2048]{2,1,0:T(8,128)(2,1)S(1)}, bf16[1,8,2048]{2,1,0:T(8,128)(2,1)S(1)}, u32[]{:S(2)}, u32[]{:S(2)}) collective-permute-start(bf16[1,8,2048]{2,1,0:T(8,128)(2,1)S(1)} %slice.151), channel_id=1, source_target_pairs={{0,4},{4,8},{8,12},{1,5},{5,9},{9,13},{2,6},{6,10},{10,14},{3,7},{... | collective-permute-start | bytes 98312 | tf_op jit(solution)/shard_map/ppermute | solution.py:14
  36.7 6.1 %collective-permute-start.4 = (bf16[1,16,2048]{2,1,0:T(8,128)(2,1)S(1)}, bf16[1,16,2048]{2,1,0:T(8,128)(2,1)S(1)}, u32[]{:S(2)}, u32[]{:S(2)}) collective-permute-start(bf16[1,16,2048]{2,1,0:T(8,128)(2,1)S(1)} %slice.153), channel_id=1, source_target_pairs={{0,4},{4,8},{8,12},{1,5},{5,9},{9,13},{2,6},{6,10},{10,14},{3,7},{... | collective-permute-start | bytes 196616 | tf_op jit(solution)/shard_map/ppermute | solution.py:14
  43.4 7.8 %collective-permute-start.5 = (bf16[1,32,2048]{2,1,0:T(8,128)(2,1)S(1)}, bf16[1,32,2048]{2,1,0:T(8,128)(2,1)S(1)}, u32[]{:S(2)}, u32[]{:S(2)}) collective-permute-start(bf16[1,32,2048]{2,1,0:T(8,128)(2,1)S(1)} %slice.155), channel_id=1, source_target_pairs={{0,4},{4,8},{8,12},{1,5},{5,9},{9,13},{2,6},{6,10},{10,14},{3,7},{... | collective-permute-start | bytes 393224 | tf_op jit(solution)/shard_map/ppermute | solution.py:14
  51.8 10.5 %collective-permute-start.6 = (bf16[1,64,2048]{2,1,0:T(8,128)(2,1)S(1)}, bf16[1,64,2048]{2,1,0:T(8,128)(2,1)S(1)}, u32[]{:S(2)}, u32[]{:S(2)}) collective-permute-start(bf16[1,64,2048]{2,1,0:T(8,128)(2,1)S(1)} %slice.157), channel_id=1, source_target_pairs={{0,4},{4,8},{8,12},{1,5},{5,9},{9,13},{2,6},{6,10},{10,14},{3,7},{... | collective-permute-start | bytes 786440 | tf_op jit(solution)/shard_map/ppermute | solution.py:14
  63.0 13.2 %collective-permute-start.7 = (bf16[1,128,2048]{2,1,0:T(8,128)(2,1)S(1)}, bf16[1,128,2048]{2,1,0:T(8,128)(2,1)S(1)}, u32[]{:S(2)}, u32[]{:S(2)}) collective-permute-start(bf16[1,128,2048]{2,1,0:T(8,128)(2,1)S(1)} %get-tuple-element.119), channel_id=1, source_target_pairs={{0,4},{4,8},{8,12},{1,5},{5,9},{9,13},{2,6},{6,10},{10,14},{3,7},{... | collective-permute-start | bytes 1572872 | tf_op jit(solution)/shard_map/ppermute | solution.py:14
  77.7 20.4 %collective-permute-start.8 = (bf16[1,256,2048]{2,1,0:T(8,128)(2,1)}, bf16[1,256,2048]{2,1,0:T(8,128)(2,1)}, u32[]{:S(2)}, u32[]{:S(2)}) collective-permute-start(bf16[1,256,2048]{2,1,0:T(8,128)(2,1)} %fusion.52), channel_id=1, source_target_pairs={{0,4},{4,8},{8,12},{1,5},{5,9},{9,13},{2,6},{6,10},{10,14},{3,7},{... | collective-permute-start | bytes 3145736 | tf_op jit(solution)/shard_map/ppermute | solution.py:14
  83.3 316.4 %reduce-scatter.3.cloned.1.call-start = ((), (), s32[]{:S(2)}) async-start(), calls=%async_computation.2 | async-start | bytes 3145728 | tf_op jit(solution)/shard_map/reduce_scatter | solution.py:83
  100.2 29.5 %collective-permute-start.9 = (bf16[1,256,2048]{2,1,0:T(8,128)(2,1)S(1)}, bf16[1,256,2048]{2,1,0:T(8,128)(2,1)S(1)}, u32[]{:S(2)}, u32[]{:S(2)}) collective-permute-start(bf16[1,256,2048]{2,1,0:T(8,128)(2,1)S(1)} %fusion.57), channel_id=1, source_target_pairs={{0,8},{4,12},{1,9},{5,13},{2,10},{6,14},{3,11},{7,15},{16,24},{20,... | collective-permute-start | bytes 3145736 | tf_op jit(solution)/shard_map/ppermute | solution.py:14
  156.3 303.8 %reduce-scatter.5.cloned.1.call-start = ((), (), s32[]{:S(2)}) async-start(), calls=%async_computation.4 | async-start | bytes 18874368 | tf_op jit(solution)/shard_map/reduce_scatter | solution.py:89
  167.9 66.6 %copy-start.29 = (bf16[1,256,2048]{2,1,0:T(8,128)(2,1)S(1)}, bf16[1,256,2048]{2,1,0:T(8,128)(2,1)}, u32[]{:S(2)}) copy-start(bf16[1,256,2048]{2,1,0:T(8,128)(2,1)} %copy-done.28) | copy-start | bytes 3145732
  167.9 66.6 %copy-start.35 = (bf16[1,256,2048]{2,1,0:T(8,128)(2,1)S(1)}, bf16[1,256,2048]{2,1,0:T(8,128)(2,1)}, u32[]{:S(2)}) copy-start(bf16[1,256,2048]{2,1,0:T(8,128)(2,1)} %copy-done.34) | copy-start | bytes 3145732
  167.9 66.6 %copy-start.36 = (bf16[1,256,2048]{2,1,0:T(8,128)(2,1)S(1)}, bf16[1,256,2048]{2,1,0:T(8,128)(2,1)}, u32[]{:S(2)}) copy-start(bf16[1,256,2048]{2,1,0:T(8,128)(2,1)} %get-tuple-element.111) | copy-start | bytes 3145732
  168.0 66.6 %copy-start.40 = (f32[1,2048]{1,0:T(1,128)S(1)}, f32[1,2048]{1,0:T(1,128)}, u32[]{:S(2)}) copy-start(f32[1,2048]{1,0:T(1,128)} %copy-done.39) | copy-start | bytes 24580
  168.0 66.6 %copy-start.43 = (f32[1,2048]{1,0:T(1,128)S(1)}, f32[1,2048]{1,0:T(1,128)}, u32[]{:S(2)}) copy-start(f32[1,2048]{1,0:T(1,128)} %copy-done.42) | copy-start | bytes 24580
  168.0 66.6 %copy-start.63 = (f32[1,2048]{1,0:T(1,128)S(1)}, f32[1,2048]{1,0:T(1,128)}, u32[]{:S(2)}) copy-start(f32[1,2048]{1,0:T(1,128)} %copy-done.62) | copy-start | bytes 24580
  168.0 66.6 %copy-start.79 = (f32[2048]{0:T(1024)S(1)}, f32[2048]{0:T(1024)}, u32[]{:S(2)}) copy-start(f32[2048]{0:T(1024)} %copy-done.78) | copy-start | bytes 24580
  168.0 66.6 %copy-start.81 = (f32[2048]{0:T(1024)S(1)}, f32[2048]{0:T(1024)}, u32[]{:S(2)}) copy-start(f32[2048]{0:T(1024)} %copy-done.80) | copy-start | bytes 24580
  179.2 55.3 %collective-permute-start.10 = (bf16[1,256,2048]{2,1,0:T(8,128)(2,1)S(1)}, bf16[1,256,2048]{2,1,0:T(8,128)(2,1)S(1)}, u32[]{:S(2)}, u32[]{:S(2)}) collective-permute-start(bf16[1,256,2048]{2,1,0:T(8,128)(2,1)S(1)} %get-tuple-element.148), channel_id=1, source_target_pairs={{8,0},{12,4},{9,1},{13,5},{10,2},{14,6},{11,3},{15,7},{24,16},{28,... | collective-permute-start | bytes 3145736 | tf_op jit(solution)/shard_map/ppermute | solution.py:14
  243.6 50.3 %collective-permute-start.11 = (bf16[1,256,2048]{2,1,0:T(8,128)(2,1)S(1)}, bf16[1,256,2048]{2,1,0:T(8,128)(2,1)S(1)}, u32[]{:S(2)}, u32[]{:S(2)}) collective-permute-start(bf16[1,256,2048]{2,1,0:T(8,128)(2,1)S(1)} %fusion.96), channel_id=1, source_target_pairs={{4,0},{8,4},{12,8},{5,1},{9,5},{13,9},{6,2},{10,6},{14,10},{7,3},{... | collective-permute-start | bytes 3145736 | tf_op jit(solution)/shard_map/ppermute | solution.py:14
  295.5 26.7 %collective-permute-start.12 = (bf16[1,128,2048]{2,1,0:T(8,128)(2,1)S(1)}, bf16[1,128,2048]{2,1,0:T(8,128)(2,1)S(1)}, u32[]{:S(2)}, u32[]{:S(2)}) collective-permute-start(bf16[1,128,2048]{2,1,0:T(8,128)(2,1)S(1)} %get-tuple-element.118), channel_id=1, source_target_pairs={{4,0},{8,4},{12,8},{5,1},{9,5},{13,9},{6,2},{10,6},{14,10},{7,3},{... | collective-permute-start | bytes 1572872 | tf_op jit(solution)/shard_map/ppermute | solution.py:14
  328.3 16.1 %collective-permute-start.13 = (bf16[1,64,2048]{2,1,0:T(8,128)(2,1)S(1)}, bf16[1,64,2048]{2,1,0:T(8,128)(2,1)S(1)}, u32[]{:S(2)}, u32[]{:S(2)}) collective-permute-start(bf16[1,64,2048]{2,1,0:T(8,128)(2,1)S(1)} %slice.164), channel_id=1, source_target_pairs={{4,0},{8,4},{12,8},{5,1},{9,5},{13,9},{6,2},{10,6},{14,10},{7,3},{... | collective-permute-start | bytes 786440 | tf_op jit(solution)/shard_map/ppermute | solution.py:14
  345.9 10.7 %collective-permute-start.14 = (bf16[1,32,2048]{2,1,0:T(8,128)(2,1)S(1)}, bf16[1,32,2048]{2,1,0:T(8,128)(2,1)S(1)}, u32[]{:S(2)}, u32[]{:S(2)}) collective-permute-start(bf16[1,32,2048]{2,1,0:T(8,128)(2,1)S(1)} %slice.166), channel_id=1, source_target_pairs={{4,0},{8,4},{12,8},{5,1},{9,5},{13,9},{6,2},{10,6},{14,10},{7,3},{... | collective-permute-start | bytes 393224 | tf_op jit(solution)/shard_map/ppermute | solution.py:14
  361.4 8.4 %collective-permute-start.15 = (bf16[1,16,2048]{2,1,0:T(8,128)(2,1)S(1)}, bf16[1,16,2048]{2,1,0:T(8,128)(2,1)S(1)}, u32[]{:S(2)}, u32[]{:S(2)}) collective-permute-start(bf16[1,16,2048]{2,1,0:T(8,128)(2,1)S(1)} %slice.168), channel_id=1, source_target_pairs={{4,0},{8,4},{12,8},{5,1},{9,5},{13,9},{6,2},{10,6},{14,10},{7,3},{... | collective-permute-start | bytes 196616 | tf_op jit(solution)/shard_map/ppermute | solution.py:14
  371.3 7.0 %collective-permute-start.16 = (bf16[1,8,2048]{2,1,0:T(8,128)(2,1)S(1)}, bf16[1,8,2048]{2,1,0:T(8,128)(2,1)S(1)}, u32[]{:S(2)}, u32[]{:S(2)}) collective-permute-start(bf16[1,8,2048]{2,1,0:T(8,128)(2,1)S(1)} %slice.170), channel_id=1, source_target_pairs={{4,0},{8,4},{12,8},{5,1},{9,5},{13,9},{6,2},{10,6},{14,10},{7,3},{... | collective-permute-start | bytes 98312 | tf_op jit(solution)/shard_map/ppermute | solution.py:14
  383.4 6.5 %collective-permute-start.17 = (bf16[1,4,2048]{2,1,0:T(4,128)(2,1)S(1)}, bf16[1,4,2048]{2,1,0:T(4,128)(2,1)S(1)}, u32[]{:S(2)}, u32[]{:S(2)}) collective-permute-start(bf16[1,4,2048]{2,1,0:T(4,128)(2,1)S(1)} %slice.172), channel_id=1, source_target_pairs={{4,0},{8,4},{12,8},{5,1},{9,5},{13,9},{6,2},{10,6},{14,10},{7,3},{... | collective-permute-start | bytes 49160 | tf_op jit(solution)/shard_map/ppermute | solution.py:14
  391.5 6.1 %collective-permute-start.18 = (bf16[1,2,2048]{2,1,0:T(2,128)(2,1)S(1)}, bf16[1,2,2048]{2,1,0:T(2,128)(2,1)S(1)}, u32[]{:S(2)}, u32[]{:S(2)}) collective-permute-start(bf16[1,2,2048]{2,1,0:T(2,128)(2,1)S(1)} %slice.348), channel_id=1, source_target_pairs={{4,0},{8,4},{12,8},{5,1},{9,5},{13,9},{6,2},{10,6},{14,10},{7,3},{... | collective-permute-start | bytes 24584 | tf_op jit(solution)/shard_map/ppermute | solution.py:14
  408.7 49.7 %collective-permute-start.19 = (bf16[1,1,2048]{2,1,0:T(2,128)(2,1)}, bf16[1,1,2048]{2,1,0:T(2,128)(2,1)S(1)}, u32[]{:S(2)}, u32[]{:S(2)}) collective-permute-start(bf16[1,1,2048]{2,1,0:T(2,128)(2,1)} %slice.350), channel_id=1, source_target_pairs={{4,0},{8,4},{12,8},{5,1},{9,5},{13,9},{6,2},{10,6},{14,10},{7,3},{... | collective-permute-start | bytes 12296 | tf_op jit(solution)/shard_map/ppermute | solution.py:14
  (134 other events, 3167.8 us)
Sparse Core Ops, SparseCore 0:
  83.4 32.3 all-gather.1
  156.4 45.6 reduce-scatter.2
  204.6 213.1 reduce-scatter.4
